TPU v7x, 256 devices: a whole 4x4x8 slice. The times are simulated.
256 devices in a mesh: section: 2 (over y_hi), grp: 4 (over x), tok: 32 (over y_lo, z, core).
Axes of the slice: x: 4, y: 4 (y_hi: 2, y_lo: 2; y = y_hi * 2 + y_lo), z: 8, core: 2. Of those that a mesh axis runs over, the one named last changes fastest.
Arguments:
- image_in: bfloat16 [2, 4, 128, 3072], P('section', 'grp', 'tok'), may hold values from -1.5 to 1.5
- text_in: bfloat16 [2, 4, 512, 3072], P('section', 'grp', 'tok'), may hold values from -1.5 to 1.5
- text_length: int32 [4], P('grp'), may hold values from 256 to 512, as said below
- entry_order: int32 [4, 4], P('grp'), may hold values from 0 to 3, as said below
- step_index: int32 [4, 4], P('grp'), may hold values from 0 to 3
- image_modulation: bfloat16 [2, 4, 18432], P('section'), may hold values from -3 to 3
- text_modulation: bfloat16 [2, 4, 9216], P('section'), may hold values from -3 to 3
- image_to_heads: bfloat16 [2, 3072, 9216], P('section', None, 'tok'), may hold values from -0.109375 to 0.109375
- text_to_heads: bfloat16 [2, 3072, 9216], P('section', None, 'tok'), may hold values from -0.109375 to 0.109375
- head_gain: float32 [2, 4, 128], P('section'), may hold values from 0.5 to 2
- image_from_heads: bfloat16 [2, 3072, 3072], P('section', None, 'tok'), may hold values from -0.109375 to 0.109375
- text_from_heads: bfloat16 [2, 3072, 3072], P('section', None, 'tok'), may hold values from -0.109375 to 0.109375
- image_up: bfloat16 [2, 3072, 12288], P('section', None, 'tok'), may hold values from -0.109375 to 0.109375
- image_down: bfloat16 [2, 12288, 3072], P('section', 'tok'), may hold values from -0.0546875 to 0.0546875
- stale_cache: bfloat16 [2, 4, 512, 6144], P('section', 'grp', 'tok'), may hold values from -400 to 400
- final_modulation: bfloat16 [4, 6144], replicated, may hold values from -3 to 3
- final_weight: bfloat16 [3072, 64], P(None, 'section'), may hold values from -0.109375 to 0.109375
- latents: float32 [4, 128, 64], P('grp', 'tok', 'section'), may hold values from -6 to 6
Outputs:
- image_handoff: bfloat16 [2, 4, 128, 3072], P('section', 'grp', 'tok')
- text_handoff: bfloat16 [2, 4, 512, 3072], P('section', 'grp', 'tok')
- fresh_cache: bfloat16 [2, 4, 512, 6144], P('section', 'grp', 'tok')
- latents_next: float32 [4, 128, 64], P('grp', 'tok', 'section')
Inputs may be any that keep to these rules, and one draw needn't show every extreme that they name: `text_length`: valid text tokens of each request; some request has exactly 512. `entry_order`: each row is a permutation of the 4 patch numbers.
All inputs are finite; a program needn't handle non-finite values.
Results may differ from a plain program's by a relative error of at most 0.023.
The roundings to bfloat16 on the way count: a program that leaves them out, or rounds other values in their place, can miss the bound.
Values may be sent and summed in bfloat16 or wider, within the bound.
No kernel may reach another device: no remote copies, remote signals or barrier semaphores. Data moves between devices by JAX's collectives and lax.ppermute only.
A program may use at most 128 MiB of HBM per device.

v0:
```python
import jax
import jax.numpy as jnp
from jax import lax
from jax.sharding import PartitionSpec as P

HDIM = 128
TSTEPS = 4
eps = 1e-06
masked_score = -1e30


def from_behind(block, axis, distance):
    devices = range(lax.axis_size(axis))
    route = [((i - distance) % len(devices), i) for i in devices]
    return lax.ppermute(block, axis, route)


def layer_norm(field):
    mean = jnp.mean(field, axis=-1, keepdims=True)
    centred = field - mean
    spread = jnp.mean(centred * centred, axis=-1, keepdims=True)
    return centred * lax.rsqrt(spread + eps)


def modulate(field, shift, scale):
    return layer_norm(field) * (1.0 + scale) + shift


def head_norm(field, gain):
    height, width = field.shape
    shaped = field.reshape(height, width // HDIM, HDIM)
    power = jnp.mean(shaped * shaped, axis=-1, keepdims=True)
    return (shaped * lax.rsqrt(power + eps) * gain).reshape(height, width)


def attend(carry, queries, piece, valid):
    highest, total, mixed = carry
    height, width = queries.shape
    heads = width // HDIM
    keys = piece[:, :width].reshape(-1, heads, HDIM)
    values = piece[:, width:].reshape(-1, heads, HDIM)
    scores = jnp.einsum(
        "qhd,khd->qhk",
        queries.reshape(height, heads, HDIM),
        keys,
        preferred_element_type=jnp.float32,
    ) * HDIM ** (-0.5)
    scores = jnp.where(valid[None, None, :], scores, masked_score)
    new_high = jnp.maximum(highest, jnp.max(scores, axis=-1))
    expo = jnp.where(valid[None, None, :], jnp.exp(scores - new_high[..., None]), 0.0)
    keep = jnp.exp(highest - new_high)
    total = total * keep + jnp.sum(expo, axis=-1)
    mixed = mixed * keep[..., None] + jnp.einsum(
        "qhk,khd->qhd", expo.astype(jnp.bfloat16), values, preferred_element_type=jnp.float32
    )
    return (new_high, total, mixed)


def empty_carry(height, heads):
    return (
        jnp.full((height, heads), masked_score, jnp.float32),
        jnp.zeros((height, heads), jnp.float32),
        jnp.zeros((height, heads, HDIM), jnp.float32),
    )


def shards(
    image_in,
    text_in,
    text_length,
    entry_order,
    step_index,
    image_modulation,
    text_modulation,
    image_to_heads,
    text_to_heads,
    head_gain,
    image_from_heads,
    text_from_heads,
    image_up,
    image_down,
    stale_cache,
    final_modulation,
    final_weight,
    latents,
):
    section = lax.axis_index("section")
    last_section = lax.axis_size("section") - 1
    position = lax.axis_index("tok")
    image_x = image_in[0, 0].astype(jnp.float32)
    text_x = text_in[0, 0].astype(jnp.float32)
    image_rows = image_x.shape[0]
    width = image_x.shape[1]
    heads = width // HDIM
    patch = lax.dynamic_index_in_dim(entry_order[0], section, 0, False)
    step_now = lax.dynamic_index_in_dim(step_index[0], patch, 0, False)
    modul = (
        lax.dynamic_index_in_dim(image_modulation[0], step_now, 0, False)
        .astype(jnp.float32)
        .reshape(6, width)
    )
    text_mod = (
        lax.dynamic_index_in_dim(text_modulation[0], step_now, 0, False)
        .astype(jnp.float32)
        .reshape(3, width)
    )
    image_normed = modulate(image_x, modul[0], modul[1]).astype(jnp.bfloat16)
    text_normed = modulate(text_x, text_mod[0], text_mod[1]).astype(jnp.bfloat16)
    every_image, every_text = (
        lax.all_gather(image_normed, "tok", axis=0, tiled=True),
        lax.all_gather(text_normed, "tok", axis=0, tiled=True),
    )
    image_cols = jnp.dot(every_image, image_to_heads[0], preferred_element_type=jnp.float32).astype(
        jnp.bfloat16
    )
    text_cols = jnp.dot(every_text, text_to_heads[0], preferred_element_type=jnp.float32).astype(
        jnp.bfloat16
    )
    image_proj, text_proj = (
        lax.all_to_all(image_cols, "tok", split_axis=0, concat_axis=1, tiled=True),
        lax.all_to_all(text_cols, "tok", split_axis=0, concat_axis=1, tiled=True),
    )
    gains = head_gain[0]
    image_query = head_norm(image_proj[:, :width].astype(jnp.float32), gains[0]).astype(
        jnp.bfloat16
    )
    image_key = head_norm(image_proj[:, width : 2 * width].astype(jnp.float32), gains[1]).astype(
        jnp.bfloat16
    )
    text_query = head_norm(text_proj[:, :width].astype(jnp.float32), gains[2]).astype(jnp.bfloat16)
    text_key = head_norm(text_proj[:, width : 2 * width].astype(jnp.float32), gains[3]).astype(
        jnp.bfloat16
    )
    fresh_image = jnp.concatenate([image_key, image_proj[:, 2 * width :]], axis=1)
    fresh_text = jnp.concatenate([text_key, text_proj[:, 2 * width :]], axis=1)
    queries = jnp.concatenate([image_query, text_query], axis=0)
    query_rows = queries.shape[0]
    patch_rows = lax.all_gather(fresh_image, "tok", axis=0, tiled=True)
    stale = stale_cache[0, 0]
    cache_rows = stale.shape[0]
    patch_len = patch_rows.shape[0]
    first_row = position * cache_rows
    begin = patch * patch_len
    offset = jnp.clip(first_row - begin, 0, patch_len - cache_rows)
    window = lax.dynamic_slice_in_dim(patch_rows, offset, cache_rows, 0)
    inside = jnp.logical_and(first_row >= begin, first_row < begin + patch_len)
    current = jnp.where(inside, window, stale)
    text_count = text_length[0]
    piece = lax.all_gather(current, "tok", axis=0, tiled=True)
    carry = attend(
        empty_carry(query_rows, heads), queries, piece, jnp.ones((piece.shape[0],), bool)
    )
    piece = lax.all_gather(fresh_text, "tok", axis=0, tiled=True)
    where_text = jnp.arange(piece.shape[0], dtype=jnp.int32)
    highest, total, mixed = attend(carry, queries, piece, where_text < text_count)
    attended = (mixed / total[..., None]).reshape(query_rows, width).astype(jnp.bfloat16)
    every_image_att, every_text_att = (
        lax.all_gather(attended[:image_rows], "tok", axis=0, tiled=True),
        lax.all_gather(attended[image_rows:], "tok", axis=0, tiled=True),
    )
    image_back_cols = jnp.dot(
        every_image_att, image_from_heads[0], preferred_element_type=jnp.float32
    ).astype(jnp.bfloat16)
    text_back_cols = jnp.dot(
        every_text_att, text_from_heads[0], preferred_element_type=jnp.float32
    ).astype(jnp.bfloat16)
    image_back, text_back = (
        lax.all_to_all(image_back_cols, "tok", split_axis=0, concat_axis=1, tiled=True),
        lax.all_to_all(text_back_cols, "tok", split_axis=0, concat_axis=1, tiled=True),
    )
    image_mid = image_x + modul[2] * image_back.astype(jnp.float32)
    text_out = (text_x + text_mod[2] * text_back.astype(jnp.float32)).astype(jnp.bfloat16)
    mlp_normed = modulate(image_mid, modul[3], modul[4]).astype(jnp.bfloat16)
    up_weight = image_up[0]
    down_weight = image_down[0]
    hidden = jax.nn.gelu(
        jnp.dot(
            lax.all_gather(mlp_normed, "tok", axis=0, tiled=True),
            up_weight,
            preferred_element_type=jnp.float32,
        ),
        approximate=True,
    ).astype(jnp.bfloat16)
    reduced = lax.psum_scatter(
        jnp.dot(hidden, down_weight, preferred_element_type=jnp.float32),
        "tok",
        scatter_dimension=0,
        tiled=True,
    )
    image_out = (image_mid + modul[5] * reduced).astype(jnp.bfloat16)
    joined = from_behind(jnp.concatenate([image_out, text_out], axis=0), "section", 1)
    image_next = joined[:image_rows]
    text_next = joined[image_rows:]
    final_source = jnp.where(section == last_section, image_out, image_next)
    patch_last = entry_order[0, last_section]
    step_last = lax.dynamic_index_in_dim(step_index[0], patch_last, 0, False)
    final_mod = (
        lax.dynamic_index_in_dim(final_modulation, step_last, 0, False)
        .astype(jnp.float32)
        .reshape(2, width)
    )
    normed = modulate(final_source.astype(jnp.float32), final_mod[0], final_mod[1]).astype(
        jnp.bfloat16
    )
    velocity = jnp.dot(normed, final_weight, preferred_element_type=jnp.float32)
    latents_next = latents[0] + -1.0 / TSTEPS * velocity
    return (image_next[None, None], text_next[None, None], current[None, None], latents_next[None])


def solution(mesh):
    placed = (
        P("section", "grp", "tok", None),
        P("section", "grp", "tok", None),
        P("grp"),
        P("grp", None),
        P("grp", None),
        P("section", None, None),
        P("section", None, None),
        P("section", None, "tok"),
        P("section", None, "tok"),
        P("section", None, None),
        P("section", None, "tok"),
        P("section", None, "tok"),
        P("section", None, "tok"),
        P("section", "tok", None),
        P("section", "grp", "tok", None),
        P(),
        P(None, "section"),
        P("grp", "tok", "section"),
    )
    return jax.shard_map(
        shards,
        mesh=mesh,
        in_specs=placed,
        out_specs=(
            P("section", "grp", "tok", None),
            P("section", "grp", "tok", None),
            P("section", "grp", "tok", None),
            P("grp", "tok", "section"),
        ),
        check_vma=False,
    )
```

profile of v0, /device:TPU:1, one launch (start us, length us, event | category | flops | bytes accessed | tf_op | source)
XLA Modules:
  0.0 711.8 jit_solution(14484903372511090327)
XLA Ops:
  20.1 40.7 %all-gather = bf16[32,4,3072]{2,1,0:T(4,128)(2,1)S(1)} all-gather(bf16[1,4,3072]{2,1,0:T(4,128)(2,1)S(1)} %fusion.94), channel_id=1, replica_groups=mesh['section'=2,'grp'=4,'tok'=32] {'tok'}, dimensions={0}, use_global_device_ids=true | all-gather | bytes 811008 | tf_op jit(solution)/shard_map/all_gather | solution.py:110
  61.9 2.4 fusion.19
  65.1 3.7 all-to-all-start
  68.8 8.5 %all-to-all-done = bf16[32,4,288]{2,1,0:T(4,128)(2,1)S(1)} async-done(((bf16[32,4,288]{2,1,0:T(4,128)(2,1)}), bf16[32,4,288]{2,1,0:T(4,128)(2,1)S(1)}, u32[]{:S(2)}, u32[]{:S(2)}) %all-to-all-start) | async-done | bytes 73760 | tf_op jit(solution)/shard_map/all_to_all | solution.py:120
  81.7 59.4 %all-gather.18.cloned.1.call-done = bf16[32,4,6144]{2,1,0:T(4,128)(2,1)} async-done(((bf16[1,4,6144]{2,1,0:T(4,128)(2,1)}), bf16[32,4,6144]{2,1,0:T(4,128)(2,1)}) %all-gather.18.cloned.1.call-update) | async-done | bytes 1572880 | tf_op jit(solution)/shard_map/all_gather | solution.py:138
  141.1 3.7 reshape.266
  144.8 1.7 bitcast_select_fusion
  146.5 62.8 %all-gather.12.cloned.1.call-done = bf16[512,3072]{1,0:T(8,128)(2,1)} async-done(((bf16[16,3072]{1,0:T(8,128)(2,1)}), bf16[512,3072]{1,0:T(8,128)(2,1)}) %all-gather.12.cloned.1.call-update) | async-done | bytes 3145744 | tf_op jit(solution)/shard_map/all_gather | solution.py:111
  209.3 3.5 fusion.11
  213.8 6.6 all-to-all-start.1
  220.5 16.5 %all-to-all-done.1 = bf16[32,16,288]{2,1,0:T(8,128)(2,1)S(1)} async-done(((bf16[32,16,288]{2,1,0:T(8,128)(2,1)}), bf16[32,16,288]{2,1,0:T(8,128)(2,1)S(1)}, u32[]{:S(2)}, u32[]{:S(2)}) %all-to-all-start.1) | async-done | bytes 294944 | tf_op jit(solution)/shard_map/all_to_all | solution.py:121
  240.4 45.5 %all-gather.10.cloned.1.call-done = bf16[512,6144]{1,0:T(8,128)(2,1)} async-done(((bf16[16,6144]{1,0:T(8,128)(2,1)}), bf16[512,6144]{1,0:T(8,128)(2,1)}) %all-gather.10.cloned.1.call-update) | async-done | bytes 6291472 | tf_op jit(solution)/shard_map/all_gather | solution.py:149
  285.8 5.9 fusion.111
  291.7 4.8 copy.82
  296.5 4.7 copy.81
  301.2 2.6 fusion.115
  303.7 53.0 %all-gather.14.cloned.1.call-done = bf16[512,6144]{1,0:T(8,128)(2,1)} async-done(((bf16[16,6144]{1,0:T(8,128)(2,1)}), bf16[512,6144]{1,0:T(8,128)(2,1)}) %all-gather.14.cloned.1.call-update) | async-done | bytes 6291472 | tf_op jit(solution)/shard_map/all_gather | solution.py:153
  356.7 6.0 fusion.110
  362.7 4.7 copy.68
  367.4 4.7 copy.70
  372.0 2.7 fusion.116
  379.4 34.4 %all-gather.2 = bf16[32,4,3072]{2,1,0:T(4,128)(2,1)S(1)} all-gather(bf16[1,4,3072]{2,1,0:T(4,128)(2,1)S(1)} %slice_bitcast_fusion.2), channel_id=1, replica_groups=mesh['section'=2,'grp'=4,'tok'=32] {'tok'}, dimensions={0}, use_global_device_ids=true | all-gather | bytes 811008 | tf_op jit(solution)/shard_map/all_gather | solution.py:158
  414.9 1.7 convolution_convert_fusion.1
  416.7 12.0 %all_to_all.64 = bf16[32,4,96]{2,1,0:T(4,128)(2,1)S(1)} all-to-all(bf16[32,4,96]{2,1,0:T(4,128)(2,1)S(1)} %bitcast.220), channel_id=1, replica_groups=mesh['section'=2,'grp'=4,'tok'=32] {'tok'}, dimensions={0} | all-to-all | bytes 49152 | tf_op jit(solution)/shard_map/all_to_all | solution.py:168
  429.3 36.7 %all-gather.3 = bf16[32,4,3072]{2,1,0:T(4,128)(2,1)} all-gather(bf16[1,4,3072]{2,1,0:T(4,128)(2,1)S(1)} %fusion.92), channel_id=1, replica_groups=mesh['section'=2,'grp'=4,'tok'=32] {'tok'}, dimensions={0}, use_global_device_ids=true | all-gather | bytes 811008 | tf_op jit(solution)/shard_map/all_gather | solution.py:178
  466.0 1.6 reshape.270
  467.6 4.0 fusion
  475.0 3.0 convolution_convert_fusion
  478.8 3.7 all-to-all-start.3
  482.5 212.0 %all-reduce.3.cloned.1.call-done = f32[128,3072]{1,0:T(8,128)} async-done(((f32[128,3072]{1,0:T(8,128)}), f32[128,3072]{1,0:T(8,128)}) %all-reduce.3.cloned.1.call-update) | async-done | bytes 1572880
  695.8 2.5 collective-permute-start
  698.4 4.1 collective-permute-done
  (137 shorter events, 28.0 us)
Async XLA Ops:
  7.2 460.4 %copy-start = (bf16[1,384,3072]{2,1,0:T(8,128)(2,1)S(1)}, bf16[1,384,3072]{2,1,0:T(8,128)(2,1)}, u32[]{:S(2)}) copy-start(bf16[1,384,3072]{2,1,0:T(8,128)(2,1)} %param.31) | copy-start | bytes 7077892
  61.9 6.9 copy-start.15
  61.9 17.3 %copy-start.3 = (bf16[1,1,16,3072]{3,2,1,0:T(8,128)(2,1)S(1)}, bf16[1,1,16,3072]{3,2,1,0:T(8,128)(2,1)}, u32[]{:S(2)}) copy-start(bf16[1,1,16,3072]{3,2,1,0:T(8,128)(2,1)} %param.19) | copy-start | bytes 294916
  61.9 17.7 %copy-start.13 = (bf16[1,4,9216]{2,1,0:T(4,128)(2,1)S(1)}, bf16[1,4,9216]{2,1,0:T(4,128)(2,1)}, u32[]{:S(2)}) copy-start(bf16[1,4,9216]{2,1,0:T(4,128)(2,1)} %param.24) | copy-start | bytes 221188
  65.1 12.2 %all-to-all-start = ((bf16[32,4,288]{2,1,0:T(4,128)(2,1)}), bf16[32,4,288]{2,1,0:T(4,128)(2,1)S(1)}, u32[]{:S(2)}, u32[]{:S(2)}) async-start(bf16[32,4,288]{2,1,0:T(4,128)(2,1)} %all_to_all.48), calls=%async_computation | async-start | bytes 196608 | tf_op jit(solution)/shard_map/all_to_all | solution.py:120
  68.7 72.4 %all-gather.18.cloned.1.call-start = ((), (), s32[]{:S(2)}) async-start(), calls=%async_computation.8 | async-start | bytes 1622016 | tf_op jit(solution)/shard_map/all_gather | solution.py:138
  79.2 130.2 %all-gather.12.cloned.1.call-start = ((), (), s32[]{:S(2)}) async-start(), calls=%async_computation.5 | async-start | bytes 3244032 | tf_op jit(solution)/shard_map/all_gather | solution.py:111
  79.6 65.1 %copy-start.7 = (bf16[1,1,16,6144]{3,2,1,0:T(8,128)(2,1)S(1)}, bf16[1,1,16,6144]{3,2,1,0:T(8,128)(2,1)}, u32[]{:S(2)}) copy-start(bf16[1,1,16,6144]{3,2,1,0:T(8,128)(2,1)} %param.32) | copy-start | bytes 589828
  81.0 204.8 %all-gather.10.cloned.1.call-start = ((), (), s32[]{:S(2)}) async-start(), calls=%async_computation.4 | async-start | bytes 6488064 | tf_op jit(solution)/shard_map/all_gather | solution.py:149
  213.8 23.1 %all-to-all-start.1 = ((bf16[32,16,288]{2,1,0:T(8,128)(2,1)}), bf16[32,16,288]{2,1,0:T(8,128)(2,1)S(1)}, u32[]{:S(2)}, u32[]{:S(2)}) async-start(bf16[32,16,288]{2,1,0:T(8,128)(2,1)} %bitcast.21), calls=%async_computation.1 | async-start | bytes 786432 | tf_op jit(solution)/shard_map/all_to_all | solution.py:121
  220.4 136.3 %all-gather.14.cloned.1.call-start = ((), (), s32[]{:S(2)}) async-start(), calls=%async_computation.6 | async-start | bytes 6488064 | tf_op jit(solution)/shard_map/all_gather | solution.py:153
  239.0 236.0 %all-gather.16.cloned.1.call-start = ((), (), s32[]{:S(2)}) async-start(), calls=%async_computation.7 | async-start | bytes 3244032 | tf_op jit(solution)/shard_map/all_gather | solution.py:159
  372.0 3.5 copy-start.1
  375.5 1.9 copy-start.2
  379.2 315.3 %all-reduce.3.cloned.1.call-start = ((), (), s32[]{:S(2)}) async-start(), calls=%async_computation.9 | async-start | bytes 3145728
  413.9 15.0 %copy-start.6 = (bf16[1,1,4,3072]{3,2,1,0:T(4,128)(2,1)S(1)}, bf16[1,1,4,3072]{3,2,1,0:T(4,128)(2,1)}, u32[]{:S(2)}) copy-start(bf16[1,1,4,3072]{3,2,1,0:T(4,128)(2,1)} %param.18) | copy-start | bytes 73732
  413.9 15.0 %copy-start.12 = (f32[1,1,3072]{2,1,0:T(1,128)S(1)}, f32[1,1,3072]{2,1,0:T(1,128)}, u32[]{:S(2)}) copy-start(f32[1,1,3072]{2,1,0:T(1,128)} %get-tuple-element.27) | copy-start | bytes 36868
  413.9 15.4 %copy-start.10 = (f32[1,1,3072]{2,1,0:T(1,128)S(1)}, f32[1,1,3072]{2,1,0:T(1,128)}, u32[]{:S(2)}) copy-start(f32[1,1,3072]{2,1,0:T(1,128)} %get-tuple-element.23) | copy-start | bytes 36868
  413.9 15.4 %copy-start.11 = (f32[1,1,3072]{2,1,0:T(1,128)S(1)}, f32[1,1,3072]{2,1,0:T(1,128)}, u32[]{:S(2)}) copy-start(f32[1,1,3072]{2,1,0:T(1,128)} %get-tuple-element.24) | copy-start | bytes 36868
  467.6 5.4 copy-start.18
  467.6 7.3 %copy-start.14 = (bf16[4,6144]{1,0:T(4,128)(2,1)S(1)}, bf16[4,6144]{1,0:T(4,128)(2,1)}, u32[]{:S(2)}) copy-start(bf16[4,6144]{1,0:T(4,128)(2,1)} %param.33) | copy-start | bytes 147460
  471.6 3.4 copy-start.5
  475.0 219.6 %copy-start.9 = (f32[1,1,3072]{2,1,0:T(1,128)S(1)}, f32[1,1,3072]{2,1,0:T(1,128)}, u32[]{:S(2)}) copy-start(f32[1,1,3072]{2,1,0:T(1,128)} %get-tuple-element.22) | copy-start | bytes 36868
  478.0 217.7 %copy-start.4 = (bf16[1,1,16,3072]{3,2,1,0:T(8,128)(2,1)S(1)}, bf16[1,1,16,3072]{3,2,1,0:T(8,128)(2,1)}, u32[]{:S(2)}) copy-start(bf16[1,1,16,3072]{3,2,1,0:T(8,128)(2,1)} %param.19) | copy-start | bytes 294916
  478.0 217.7 %copy-start.8 = (f32[1,1,3072]{2,1,0:T(1,128)S(1)}, f32[1,1,3072]{2,1,0:T(1,128)}, u32[]{:S(2)}) copy-start(f32[1,1,3072]{2,1,0:T(1,128)} %get-tuple-element.32) | copy-start | bytes 36868
  478.0 224.8 %copy-start.16 = (bf16[3072,32]{0,1:T(8,128)(2,1)S(1)}, bf16[3072,32]{0,1:T(8,128)(2,1)}, u32[]{:S(2)}) copy-start(bf16[3072,32]{0,1:T(8,128)(2,1)} %param.34) | copy-start | bytes 589828
  478.0 224.8 %copy-start.17 = (f32[1,4,32]{2,1,0:T(4,128)S(1)}, f32[1,4,32]{2,1,0:T(4,128)}, u32[]{:S(2)}) copy-start(f32[1,4,32]{2,1,0:T(4,128)} %param.35) | copy-start | bytes 1540
  478.8 216.6 %all-to-all-start.3 = ((bf16[32,16,96]{2,1,0:T(8,128)(2,1)}), bf16[32,16,96]{2,1,0:T(8,128)(2,1)S(1)}, u32[]{:S(2)}, u32[]{:S(2)}) async-start(bf16[32,16,96]{2,1,0:T(8,128)(2,1)} %bitcast.47), calls=%async_computation.3 | async-start | bytes 262144 | tf_op jit(solution)/shard_map/all_to_all | solution.py:169
  695.8 6.6 collective-permute-start
Sparse Core Ops, SparseCore 0:
  79.3 61.7 all-gather.17
  143.5 65.7 all-gather.11
  211.8 74.0 all-gather.9
  287.5 69.1 all-gather.13
  379.3 66.5 all-gather.15
  471.8 222.6 all-reduce.2
where the time goes:
time: 713 us; the launch traced here: 712 us
  waiting for transfers between devices  462 us (65%)
  blocking collectives  124 us (17%)
  local copies, waits for them, and re-layouts  49.3 us (7%)
  between operations  24.4 us (3%)
  matrix products  22.6 us (3%)
  starting transfers between devices  16.9 us (2%)
  other arithmetic  13 us (2%)
    unnamed x7, waiting for transfers between devices  212 us
    all_gather x1, waiting for transfers between devices, shards(): lax.all_gather(text_normed, 'tok', axis=0, tiled=True)  62.8 us
    all_gather x1, waiting for transfers between devices, shards(): patch_rows = lax.all_gather(fresh_image, 'tok', axis=0, tiled=True)  59.4 us
    all_gather x1, waiting for transfers between devices, shards(): piece = lax.all_gather(fresh_text, 'tok', axis=0, tiled=True)  53 us
    all_gather x1, waiting for transfers between devices, shards(): piece = lax.all_gather(current, 'tok', axis=0, tiled=True)  45.5 us
    all_gather x1, blocking collectives, shards(): lax.all_gather(image_normed, 'tok', axis=0, tiled=True)  40.7 us
    all_gather x1, blocking collectives, shards(): lax.all_gather(mlp_normed, 'tok', axis=0, tiled=True)  36.7 us
    all_gather x1, blocking collectives, shards(): lax.all_gather(attended[:image_rows], 'tok', axis=0, tiled=True)  34.4 us
  transfers between devices with their start and end apart: 10, of which 8 were waited for; matrix products, arithmetic and copies ran while one was open for 6% of the time, Pallas kernels for 0%

commit v1 on v0

--- a/solution.py
+++ b/solution.py
@@ -1,3 +1,4 @@
+import functools
 import jax
 import jax.numpy as jnp
 from jax import lax
@@ -7,6 +8,17 @@
 TSTEPS = 4
 eps = 1e-06
 masked_score = -1e30
+
+
+def lay_region(piece_in, axis_key, at_axis):
+    x_next = jnp.concatenate(
+        lax.all_to_all(jnp.stack([piece_in] * lax.axis_size(axis_key)), axis_key, 0, 0),
+        axis=at_axis,
+    )
+    return x_next
+
+
+spots_close = functools.partial(lay_region, axis_key="tok", at_axis=0)
 
 
 def from_behind(block, axis, distance):
@@ -155,7 +167,7 @@
     highest, total, mixed = attend(carry, queries, piece, where_text < text_count)
     attended = (mixed / total[..., None]).reshape(query_rows, width).astype(jnp.bfloat16)
     every_image_att, every_text_att = (
-        lax.all_gather(attended[:image_rows], "tok", axis=0, tiled=True),
+        spots_close(attended[:image_rows]),
         lax.all_gather(attended[image_rows:], "tok", axis=0, tiled=True),
     )
     image_back_cols = jnp.dot(

time: 713 us -> 713 us (level)
    all_gather x1 -> x0, blocking collectives: 34.4 us -> none  [shards(): lax.all_gather(attended[:image_rows], 'tok', axis=0, tiled=True)]
    all_to_all x0 -> x1, blocking collectives: none -> 31.3 us  [lay_region(): lax.all_to_all(jnp.stack([piece_in] * lax.axis_size(axis_key)), axis_key,...]
    unnamed x50 -> x48, local copies, waits for them, and re-layouts: 18.7 us -> 17.6 us
where the time goes in v1:
time: 713 us; the launch traced here: 711 us
  waiting for transfers between devices  462 us (65%)
  blocking collectives  123 us (17%)
  local copies, waits for them, and re-layouts  49.5 us (7%)
  between operations  24.4 us (3%)
  matrix products  22.6 us (3%)
  starting transfers between devices  16.9 us (2%)
  other arithmetic  13 us (2%)
    unnamed x7, waiting for transfers between devices  213 us
    all_gather x1, waiting for transfers between devices, shards(): lax.all_gather(text_normed, 'tok', axis=0, tiled=True)  62.8 us
    all_gather x1, waiting for transfers between devices, shards(): patch_rows = lax.all_gather(fresh_image, 'tok', axis=0, tiled=True)  59.4 us
    all_gather x1, waiting for transfers between devices, shards(): piece = lax.all_gather(fresh_text, 'tok', axis=0, tiled=True)  53 us
    all_gather x1, waiting for transfers between devices, shards(): piece = lax.all_gather(current, 'tok', axis=0, tiled=True)  45.5 us
    all_gather x1, blocking collectives, shards(): lax.all_gather(image_normed, 'tok', axis=0, tiled=True)  40.7 us
    all_gather x1, blocking collectives, shards(): lax.all_gather(mlp_normed, 'tok', axis=0, tiled=True)  36.6 us
    all_to_all x1, blocking collectives, lay_region(): lax.all_to_all(jnp.stack([piece_in] * lax.axis_size(axis_key)), axis_key,...  31.3 us
  transfers between devices with their start and end apart: 10, of which 8 were waited for; matrix products, arithmetic and copies ran while one was open for 6% of the time, Pallas kernels for 0%

profile of v1, /device:TPU:1, one launch (start us, length us, event | category | flops | bytes accessed | tf_op | source)
XLA Modules:
  0.0 711.4 jit_solution(941385080455554234)
XLA Ops:
  20.1 40.7 %all-gather = bf16[32,4,3072]{2,1,0:T(4,128)(2,1)S(1)} all-gather(bf16[1,4,3072]{2,1,0:T(4,128)(2,1)S(1)} %fusion.94), channel_id=1, replica_groups=mesh['section'=2,'grp'=4,'tok'=32] {'tok'}, dimensions={0}, use_global_device_ids=true | all-gather | bytes 811008 | tf_op jit(solution)/shard_map/all_gather | solution.py:122
  61.9 2.4 fusion.19
  65.1 3.7 all-to-all-start
  68.8 8.5 %all-to-all-done = bf16[32,4,288]{2,1,0:T(4,128)(2,1)S(1)} async-done(((bf16[32,4,288]{2,1,0:T(4,128)(2,1)}), bf16[32,4,288]{2,1,0:T(4,128)(2,1)S(1)}, u32[]{:S(2)}, u32[]{:S(2)}) %all-to-all-start) | async-done | bytes 73760 | tf_op jit(solution)/shard_map/all_to_all | solution.py:132
  81.7 59.4 %all-gather.17.cloned.1.call-done = bf16[32,4,6144]{2,1,0:T(4,128)(2,1)} async-done(((bf16[1,4,6144]{2,1,0:T(4,128)(2,1)}), bf16[32,4,6144]{2,1,0:T(4,128)(2,1)}) %all-gather.17.cloned.1.call-update) | async-done | bytes 1572880 | tf_op jit(solution)/shard_map/all_gather | solution.py:150
  141.1 3.7 reshape.272
  144.8 1.7 bitcast_select_fusion
  146.5 62.8 %all-gather.11.cloned.1.call-done = bf16[512,3072]{1,0:T(8,128)(2,1)} async-done(((bf16[16,3072]{1,0:T(8,128)(2,1)}), bf16[512,3072]{1,0:T(8,128)(2,1)}) %all-gather.11.cloned.1.call-update) | async-done | bytes 3145744 | tf_op jit(solution)/shard_map/all_gather | solution.py:123
  209.3 3.5 fusion.11
  213.8 6.6 all-to-all-start.1
  220.5 16.5 %all-to-all-done.1 = bf16[32,16,288]{2,1,0:T(8,128)(2,1)S(1)} async-done(((bf16[32,16,288]{2,1,0:T(8,128)(2,1)}), bf16[32,16,288]{2,1,0:T(8,128)(2,1)S(1)}, u32[]{:S(2)}, u32[]{:S(2)}) %all-to-all-start.1) | async-done | bytes 294944 | tf_op jit(solution)/shard_map/all_to_all | solution.py:133
  240.4 45.5 %all-gather.9.cloned.1.call-done = bf16[512,6144]{1,0:T(8,128)(2,1)} async-done(((bf16[16,6144]{1,0:T(8,128)(2,1)}), bf16[512,6144]{1,0:T(8,128)(2,1)}) %all-gather.9.cloned.1.call-update) | async-done | bytes 6291472 | tf_op jit(solution)/shard_map/all_gather | solution.py:161
  285.8 5.9 fusion.111
  291.7 4.8 copy.82
  296.5 4.7 copy.81
  301.2 2.6 fusion.115
  303.7 53.0 %all-gather.13.cloned.1.call-done = bf16[512,6144]{1,0:T(8,128)(2,1)} async-done(((bf16[16,6144]{1,0:T(8,128)(2,1)}), bf16[512,6144]{1,0:T(8,128)(2,1)}) %all-gather.13.cloned.1.call-update) | async-done | bytes 6291472 | tf_op jit(solution)/shard_map/all_gather | solution.py:165
  356.7 6.0 fusion.110
  362.7 4.7 copy.68
  367.4 4.7 copy.70
  372.0 2.7 fusion.116
  379.6 31.3 %all_to_all.69 = bf16[32,4,3072]{2,1,0:T(4,128)(2,1)S(1)} all-to-all(bf16[32,4,3072]{2,1,0:T(4,128)(2,1)S(1)} %stack.2), channel_id=1, replica_groups=mesh['section'=2,'grp'=4,'tok'=32] {'tok'}, dimensions={0} | all-to-all | bytes 1572864 | tf_op jit(solution)/shard_map/all_to_all | solution.py:15
  412.0 1.7 convolution_convert_fusion.1
  413.8 14.0 %all_to_all.70 = bf16[32,4,96]{2,1,0:T(4,128)(2,1)S(1)} all-to-all(bf16[32,4,96]{2,1,0:T(4,128)(2,1)S(1)} %bitcast.220), channel_id=1, replica_groups=mesh['section'=2,'grp'=4,'tok'=32] {'tok'}, dimensions={0} | all-to-all | bytes 49152 | tf_op jit(solution)/shard_map/all_to_all | solution.py:180
  428.4 36.6 %all-gather.2 = bf16[32,4,3072]{2,1,0:T(4,128)(2,1)} all-gather(bf16[1,4,3072]{2,1,0:T(4,128)(2,1)S(1)} %fusion.92), channel_id=1, replica_groups=mesh['section'=2,'grp'=4,'tok'=32] {'tok'}, dimensions={0}, use_global_device_ids=true | all-gather | bytes 811008 | tf_op jit(solution)/shard_map/all_gather | solution.py:190
  465.0 1.6 reshape.274
  466.6 4.0 fusion
  474.0 3.0 convolution_convert_fusion
  477.8 3.7 all-to-all-start.4
  481.5 212.6 %all-reduce.3.cloned.1.call-done = f32[128,3072]{1,0:T(8,128)} async-done(((f32[128,3072]{1,0:T(8,128)}), f32[128,3072]{1,0:T(8,128)}) %all-reduce.3.cloned.1.call-update) | async-done | bytes 1572880
  695.4 2.5 collective-permute-start
  697.9 4.1 collective-permute-done
  (138 shorter events, 28.2 us)
Async XLA Ops:
  7.2 459.4 %copy-start = (bf16[1,384,3072]{2,1,0:T(8,128)(2,1)S(1)}, bf16[1,384,3072]{2,1,0:T(8,128)(2,1)}, u32[]{:S(2)}) copy-start(bf16[1,384,3072]{2,1,0:T(8,128)(2,1)} %param.31) | copy-start | bytes 7077892
  61.9 6.9 copy-start.15
  61.9 17.3 %copy-start.3 = (bf16[1,1,16,3072]{3,2,1,0:T(8,128)(2,1)S(1)}, bf16[1,1,16,3072]{3,2,1,0:T(8,128)(2,1)}, u32[]{:S(2)}) copy-start(bf16[1,1,16,3072]{3,2,1,0:T(8,128)(2,1)} %param.19) | copy-start | bytes 294916
  61.9 17.7 %copy-start.13 = (bf16[1,4,9216]{2,1,0:T(4,128)(2,1)S(1)}, bf16[1,4,9216]{2,1,0:T(4,128)(2,1)}, u32[]{:S(2)}) copy-start(bf16[1,4,9216]{2,1,0:T(4,128)(2,1)} %param.24) | copy-start | bytes 221188
  65.1 12.2 %all-to-all-start = ((bf16[32,4,288]{2,1,0:T(4,128)(2,1)}), bf16[32,4,288]{2,1,0:T(4,128)(2,1)S(1)}, u32[]{:S(2)}, u32[]{:S(2)}) async-start(bf16[32,4,288]{2,1,0:T(4,128)(2,1)} %all_to_all.51), calls=%async_computation | async-start | bytes 196608 | tf_op jit(solution)/shard_map/all_to_all | solution.py:132
  68.7 72.4 %all-gather.17.cloned.1.call-start = ((), (), s32[]{:S(2)}) async-start(), calls=%async_computation.9 | async-start | bytes 1622016 | tf_op jit(solution)/shard_map/all_gather | solution.py:150
  79.2 130.2 %all-gather.11.cloned.1.call-start = ((), (), s32[]{:S(2)}) async-start(), calls=%async_computation.6 | async-start | bytes 3244032 | tf_op jit(solution)/shard_map/all_gather | solution.py:123
  79.6 65.1 %copy-start.7 = (bf16[1,1,16,6144]{3,2,1,0:T(8,128)(2,1)S(1)}, bf16[1,1,16,6144]{3,2,1,0:T(8,128)(2,1)}, u32[]{:S(2)}) copy-start(bf16[1,1,16,6144]{3,2,1,0:T(8,128)(2,1)} %param.32) | copy-start | bytes 589828
  81.0 204.8 %all-gather.9.cloned.1.call-start = ((), (), s32[]{:S(2)}) async-start(), calls=%async_computation.5 | async-start | bytes 6488064 | tf_op jit(solution)/shard_map/all_gather | solution.py:161
  213.8 23.1 %all-to-all-start.1 = ((bf16[32,16,288]{2,1,0:T(8,128)(2,1)}), bf16[32,16,288]{2,1,0:T(8,128)(2,1)S(1)}, u32[]{:S(2)}, u32[]{:S(2)}) async-start(bf16[32,16,288]{2,1,0:T(8,128)(2,1)} %bitcast.21), calls=%async_computation.1 | async-start | bytes 786432 | tf_op jit(solution)/shard_map/all_to_all | solution.py:133
  220.4 136.3 %all-gather.13.cloned.1.call-start = ((), (), s32[]{:S(2)}) async-start(), calls=%async_computation.7 | async-start | bytes 6488064 | tf_op jit(solution)/shard_map/all_gather | solution.py:165
  239.0 235.0 %all-gather.15.cloned.1.call-start = ((), (), s32[]{:S(2)}) async-start(), calls=%async_computation.8 | async-start | bytes 3244032 | tf_op jit(solution)/shard_map/all_gather | solution.py:171
  372.0 3.5 copy-start.1
  375.5 1.9 copy-start.2
  379.2 314.9 %all-reduce.3.cloned.1.call-start = ((), (), s32[]{:S(2)}) async-start(), calls=%async_computation.10 | async-start | bytes 3145728
  410.9 17.0 %copy-start.6 = (bf16[1,1,4,3072]{3,2,1,0:T(4,128)(2,1)S(1)}, bf16[1,1,4,3072]{3,2,1,0:T(4,128)(2,1)}, u32[]{:S(2)}) copy-start(bf16[1,1,4,3072]{3,2,1,0:T(4,128)(2,1)} %param.18) | copy-start | bytes 73732
  410.9 17.0 %copy-start.12 = (f32[1,1,3072]{2,1,0:T(1,128)S(1)}, f32[1,1,3072]{2,1,0:T(1,128)}, u32[]{:S(2)}) copy-start(f32[1,1,3072]{2,1,0:T(1,128)} %get-tuple-element.27) | copy-start | bytes 36868
  410.9 17.4 %copy-start.10 = (f32[1,1,3072]{2,1,0:T(1,128)S(1)}, f32[1,1,3072]{2,1,0:T(1,128)}, u32[]{:S(2)}) copy-start(f32[1,1,3072]{2,1,0:T(1,128)} %get-tuple-element.23) | copy-start | bytes 36868
  410.9 17.4 %copy-start.11 = (f32[1,1,3072]{2,1,0:T(1,128)S(1)}, f32[1,1,3072]{2,1,0:T(1,128)}, u32[]{:S(2)}) copy-start(f32[1,1,3072]{2,1,0:T(1,128)} %get-tuple-element.24) | copy-start | bytes 36868
  466.6 5.4 copy-start.18
  466.6 7.3 %copy-start.14 = (bf16[4,6144]{1,0:T(4,128)(2,1)S(1)}, bf16[4,6144]{1,0:T(4,128)(2,1)}, u32[]{:S(2)}) copy-start(bf16[4,6144]{1,0:T(4,128)(2,1)} %param.33) | copy-start | bytes 147460
  470.7 3.4 copy-start.5
  474.0 220.1 %copy-start.9 = (f32[1,1,3072]{2,1,0:T(1,128)S(1)}, f32[1,1,3072]{2,1,0:T(1,128)}, u32[]{:S(2)}) copy-start(f32[1,1,3072]{2,1,0:T(1,128)} %get-tuple-element.22) | copy-start | bytes 36868
  477.0 218.3 %copy-start.4 = (bf16[1,1,16,3072]{3,2,1,0:T(8,128)(2,1)S(1)}, bf16[1,1,16,3072]{3,2,1,0:T(8,128)(2,1)}, u32[]{:S(2)}) copy-start(bf16[1,1,16,3072]{3,2,1,0:T(8,128)(2,1)} %param.19) | copy-start | bytes 294916
  477.0 218.3 %copy-start.8 = (f32[1,1,3072]{2,1,0:T(1,128)S(1)}, f32[1,1,3072]{2,1,0:T(1,128)}, u32[]{:S(2)}) copy-start(f32[1,1,3072]{2,1,0:T(1,128)} %get-tuple-element.32) | copy-start | bytes 36868
  477.0 225.4 %copy-start.16 = (bf16[3072,32]{0,1:T(8,128)(2,1)S(1)}, bf16[3072,32]{0,1:T(8,128)(2,1)}, u32[]{:S(2)}) copy-start(bf16[3072,32]{0,1:T(8,128)(2,1)} %param.34) | copy-start | bytes 589828
  477.0 225.4 %copy-start.17 = (f32[1,4,32]{2,1,0:T(4,128)S(1)}, f32[1,4,32]{2,1,0:T(4,128)}, u32[]{:S(2)}) copy-start(f32[1,4,32]{2,1,0:T(4,128)} %param.35) | copy-start | bytes 1540
  477.8 217.2 %all-to-all-start.4 = ((bf16[32,16,96]{2,1,0:T(8,128)(2,1)}), bf16[32,16,96]{2,1,0:T(8,128)(2,1)S(1)}, u32[]{:S(2)}, u32[]{:S(2)}) async-start(bf16[32,16,96]{2,1,0:T(8,128)(2,1)} %bitcast.47), calls=%async_computation.4 | async-start | bytes 262144 | tf_op jit(solution)/shard_map/all_to_all | solution.py:181
  695.4 6.6 collective-permute-start
Sparse Core Ops, SparseCore 0:
  79.3 61.7 all-gather.16
  143.5 65.7 all-gather.10
  211.8 74.0 all-gather.8
  287.5 69.1 all-gather.12
  379.3 70.2 all-gather.14
  470.8 223.2 all-reduce.2
